TPU v7x, 512 devices: a whole 4x8x8 slice. The times are simulated.
512 devices in a mesh: segment: 4 (over z_lo), seq: 16 (over z_hi, x, core), mp: 8 (over y).
Axes of the slice: x: 4, y: 8, z: 8 (z_hi: 2, z_lo: 4; z = z_hi * 4 + z_lo), core: 2. Of those that a mesh axis runs over, the one named last changes fastest.
Arguments:
- latents: bfloat16 [4, 16, 256, 4096], P('segment', 'seq', None, 'mp'), may hold values from -6 to 6
- w_qkv: bfloat16 [4, 4096, 3, 4096], P('segment', 'seq', None, 'mp'), may hold values from -1 to 1
- w_out: bfloat16 [4, 4096, 4096], P('segment', 'mp', 'seq'), may hold values from -0.09375 to 0.09375
- mod_shift: float32 [4, 4096], P('segment'), may hold values from -3 to 3
- mod_scale: float32 [4, 4096], P('segment'), may hold values from 0.1 to 1.9
- mod_gate: float32 [4, 4096], P('segment'), may hold values from 0.5 to 1.5
- counts: int32 [4, 16], P('segment'), may hold values from 64 to 256, as said below
Outputs:
- next_latents: bfloat16 [4, 16, 256, 4096], P('segment', 'seq', None, 'mp')
Inputs may be any that keep to these rules, and one draw needn't show every extreme that they name: `counts`: in every section's clip at least one frame has all 256 patch positions valid.
All inputs are finite; a program needn't handle non-finite values.
Results may differ from a plain program's by a relative error of at most 0.01.
Values may be sent and summed in bfloat16 or wider, within the bound.
No kernel may reach another device: no remote copies, remote signals or barrier semaphores. Data moves between devices by JAX's collectives and lax.ppermute only.
A program may use at most 64 MiB of HBM per device.

v0:
```python
import math
import jax
import jax.numpy as jnp
from jax import lax
from jax.sharding import PartitionSpec as P

HD = 128
EPS = 1e-06
NEG_FILL = -1e30


def passed_along(x, axis, by):
    length = lax.axis_size(axis)
    return lax.ppermute(x, axis, [(i, (i + by) % length) for i in range(length)])


def masked_attention(queries, keys_in, values, usable):
    factor = 1.0 / math.sqrt(queries.shape[-1])
    scores = (
        jnp.einsum("...ihe,...jhe->...hij", queries, keys_in, preferred_element_type=jnp.float32)
        * factor
    )
    allowed = usable[..., None, :, None] & usable[..., None, None, :]
    masked = jnp.where(allowed, scores, NEG_FILL)
    highest = jnp.max(masked, axis=-1, keepdims=True)
    raised = jnp.where(allowed, jnp.exp(masked - highest), 0.0)
    spare_one = jnp.where(usable, 0.0, 1.0)[..., None, :, None]
    weights = (raised / (jnp.sum(raised, axis=-1, keepdims=True) + spare_one)).astype(jnp.bfloat16)
    blended = jnp.einsum(
        "...hij,...jhe->...ihe", weights, values, preferred_element_type=jnp.float32
    )
    return blended.astype(jnp.bfloat16)


SEQ = ("zh", "x", "c")


def seq_index():
    return (lax.axis_index("zh") * lax.axis_size("x") + lax.axis_index("x")) * lax.axis_size(
        "c"
    ) + lax.axis_index("c")


def gather_seq(block):
    across = lax.all_gather(block, "zh", axis=0)
    along = lax.all_gather(across, "x", axis=1)
    both = lax.all_gather(along, "c", axis=2)
    return both.reshape((-1,) + block.shape[1:])


def relay_features(rows_now):
    return lax.all_to_all(rows_now, SEQ, split_axis=0, concat_axis=0, tiled=True)


def pass_onward(rows_now):
    return passed_along(rows_now, "segment", 1)


def on_device(latents, w_qkv, w_out, mod_shift, mod_scale, mod_gate, counts):
    frames = lax.axis_size(SEQ)
    patches = latents.shape[2]
    narrow = latents.shape[3]
    span = patches // frames
    segment_rows = latents[0, 0]
    gathered = lax.all_gather(latents, "mp", axis=3, tiled=True)[0, 0]
    widened = gathered.astype(jnp.float32)
    average = jnp.mean(widened, axis=-1, keepdims=True)
    centred = widened - average
    variance = jnp.mean(centred * centred, axis=-1, keepdims=True)
    modulated = (centred * lax.rsqrt(variance + EPS) * mod_scale[0] + mod_shift[0]).astype(
        jnp.bfloat16
    )
    columns = w_qkv.shape[2] * w_qkv.shape[3]
    piece = gather_seq(w_qkv[0])
    height = piece.shape[0]
    projected = jnp.dot(
        modulated, piece.reshape(height, columns), preferred_element_type=jnp.float32
    )
    local_heads = w_qkv.shape[3] // HD
    projected = projected.astype(jnp.bfloat16).reshape(patches, 3, local_heads, HD)
    frame_here = seq_index()
    clip_counts = counts[0]
    positions = jnp.arange(frames)

    def spatial(triple):
        count_here = jnp.sum(jnp.where(positions == frame_here, clip_counts, 0))
        usable = jnp.arange(patches) < count_here
        return masked_attention(triple[:, 0], triple[:, 1], triple[:, 2], usable)

    def temporal(triple):
        by_place = triple.reshape(frames, span, 3, local_heads, HD).transpose(1, 0, 2, 3, 4)
        location = frame_here * span + jnp.arange(span)
        usable = location[:, None] < clip_counts[None, :]
        blended = masked_attention(by_place[:, :, 0], by_place[:, :, 1], by_place[:, :, 2], usable)
        return blended.transpose(1, 0, 2, 3).reshape(patches, local_heads, HD)

    attended = lax.cond(lax.axis_index("segment") % 2 == 0, spatial, temporal, projected)
    attended = attended.reshape(patches, local_heads * HD)
    out_blocks = gather_seq(w_out[0][None])
    member = lax.axis_index("mp")
    partials = jnp.einsum(
        "tr,brc->tbc", attended, out_blocks, preferred_element_type=jnp.float32
    ).reshape(patches, -1)
    summed = lax.psum_scatter(
        partials.astype(jnp.bfloat16), "mp", scatter_dimension=1, tiled=True
    ).astype(jnp.float32)
    gate_here = lax.dynamic_slice_in_dim(mod_gate[0], member * narrow, narrow)
    updated = (segment_rows.astype(jnp.float32) + gate_here * summed).astype(jnp.bfloat16)
    updated = updated.reshape(frames, span, narrow)
    moved = pass_onward(relay_features(updated))
    return moved.reshape(1, 1, patches, narrow)


def solution(mesh):
    seg, seq, mp = mesh.devices.shape
    inner = mesh.devices.reshape(seg, 2, seq // 4, 2, mp)
    fine = jax.sharding.Mesh(inner, ("segment", "zh", "x", "c", "mp"))
    return jax.shard_map(
        on_device,
        mesh=fine,
        in_specs=(
            P("segment", SEQ, None, "mp"),
            P("segment", SEQ, None, "mp"),
            P("segment", "mp", SEQ),
            P("segment", None),
            P("segment", None),
            P("segment", None),
            P("segment", None),
        ),
        out_specs=P("segment", SEQ, None, "mp"),
        check_vma=False,
    )
```

profile of v0, /device:TPU:1, one launch (start us, length us, event | category | flops | bytes accessed | tf_op | source)
XLA Modules:
  0.0 409.4 jit_solution(5378004970461024760)
XLA Ops:
  6.5 0.0 copy-start
  6.5 0.0 all-gather.14.cloned.1.call-start
  6.5 0.7 all-gather.14.cloned.1.call-update
  7.3 0.0 all-gather.20.cloned.1.call-start
  7.3 19.6 %all-gather.2 = bf16[2,512,256]{2,1,0:T(8,128)(2,1)} all-gather(bf16[1,512,256]{2,1,0:T(8,128)(2,1)} %param.11), channel_id=4, replica_groups=mesh['segment'=4,'zh'=2,'x'=4,'c'=2,'mp'=8] {'zh'}, dimensions={0}, use_global_device_ids=true | all-gather | bytes 786432 | tf_op jit(solution)/shard_map/all_gather | solution.py:45
  26.9 0.0 all-gather.20.cloned.1.call-update
  26.9 0.0 all-gather.16.cloned.1.call-start
  26.9 44.4 %all-gather.14.cloned.1.call-done = bf16[2,256,3,512]{3,1,2,0:T(8,128)(2,1)} async-done(((bf16[1,256,3,512]{3,1,2,0:T(8,128)(2,1)}), bf16[2,256,3,512]{3,1,2,0:T(8,128)(2,1)}) %all-gather.14.cloned.1.call-update) | async-done | bytes 1572880 | tf_op jit(solution)/shard_map/all_gather | solution.py:45
  71.4 0.0 all-gather.16.cloned.1.call-update
  71.4 0.0 all-gather.12.cloned.1.call-start
  71.4 0.5 all-gather.12.cloned.1.call-update
  72.0 0.0 all-gather.22.cloned.1.call-start
  72.0 34.1 %all-gather.20.cloned.1.call-done = bf16[2,2048,256]{2,1,0:T(8,128)(2,1)} async-done(((bf16[2,512,256]{2,1,0:T(8,128)(2,1)}), bf16[2,2048,256]{2,1,0:T(8,128)(2,1)}) %all-gather.20.cloned.1.call-update) | async-done | bytes 2097168 | tf_op jit(solution)/shard_map/all_gather | solution.py:46
  106.1 0.0 all-gather.22.cloned.1.call-update
  106.2 0.0 all-gather.18.cloned.1.call-start
  106.2 73.1 %all-gather.16.cloned.1.call-done = bf16[2,1024,3,512]{3,1,2,0:T(8,128)(2,1)} async-done(((bf16[2,256,3,512]{3,1,2,0:T(8,128)(2,1)}), bf16[2,1024,3,512]{3,1,2,0:T(8,128)(2,1)}) %all-gather.16.cloned.1.call-update) | async-done | bytes 6291472 | tf_op jit(solution)/shard_map/all_gather | solution.py:46
  179.3 11.4 %copy.28 = bf16[2,4,256,3,512]{2,1,0,4,3:T(4,128)(2,1)} copy(bf16[2,4,256,3,512]{4,2,1,3,0:T(8,128)(2,1)} %bitcast.90) | data formatting | bytes 12582912 | tf_op jit(solution)/shard_map/all_gather | solution.py:46
  190.8 0.0 all-gather.18.cloned.1.call-update
  190.8 0.0 reduce-scatter.2.cloned.1.call-start
  190.8 30.5 %all-gather.12.cloned.1.call-done = bf16[1,1,256,4096]{3,2,1,0:T(8,128)(2,1)} async-done(((bf16[1,1,256,512]{3,2,1,0:T(8,128)(2,1)}), bf16[1,1,256,4096]{3,2,1,0:T(8,128)(2,1)}) %all-gather.12.cloned.1.call-update) | async-done | bytes 2097168 | tf_op jit(solution)/shard_map/all_gather | solution.py:65
  221.4 2.0 convert_reduce_fusion
  223.3 2.3 fusion.30
  225.6 23.9 %all-gather.22.cloned.1.call-done = bf16[2,4,2,512,256]{4,3,2,1,0:T(8,128)(2,1)} async-done(((bf16[2,4,1,512,256]{4,3,2,1,0:T(8,128)(2,1)}), bf16[2,4,2,512,256]{4,3,2,1,0:T(8,128)(2,1)}) %all-gather.22.cloned.1.call-update) | async-done | bytes 4194320 | tf_op jit(solution)/shard_map/all_gather | solution.py:47
  249.5 6.4 %copy.30 = bf16[16,256,512]{2,1,0:T(8,128)(2,1)} copy(bf16[16,256,512]{1,2,0:T(8,128)(2,1)} %bitcast.91) | data formatting | bytes 8388608 | tf_op jit(solution)/shard_map/tr,brc->tbc/dot_general | solution.py:101
  255.9 0.0 copy-start.1
  255.9 0.0 copy-start.4
  255.9 0.0 copy-start.5
  255.9 29.7 %all-gather.18.cloned.1.call-done = bf16[2,4,512,3,512]{2,1,0,4,3:T(4,128)(2,1)} async-done(((bf16[2,4,256,3,512]{2,1,0,4,3:T(4,128)(2,1)}), bf16[2,4,512,3,512]{2,1,0,4,3:T(4,128)(2,1)}) %all-gather.18.cloned.1.call-update) | async-done | bytes 12582928 | tf_op jit(solution)/shard_map/all_gather | solution.py:47
  285.6 21.0 %reshape_reshape.6 = bf16[4096,1536]{0,1:T(8,128)(2,1)} reshape(bf16[2,4,512,3,512]{2,1,0,4,3:T(4,128)(2,1)} %all-gather.18.cloned.1.call-done) | data formatting | bytes 25165824 | tf_op jit(solution)/shard_map/reshape;reshape | solution.py:77
  306.6 0.0 copy-done.1
  306.6 0.0 copy-done.4
  306.6 0.0 copy-done.5
  306.6 0.0 copy-start.3
  306.6 8.1 %convolution_convert_fusion.3 = bf16[256,1536]{1,0:T(8,128)(2,1)S(1)} fusion(bf16[4096,1536]{0,1:T(8,128)(2,1)} %reshape_reshape.6, bf16[1,1,256,4096]{3,2,1,0:T(8,128)(2,1)S(1)} %copy-done.1, f32[4096]{0:T(1024)S(1)} %bitcast.105, f32[4096]{0:T(1024)S(1)} %bitcast.106, f32[256]{0:T(256)S(1)} %add_rsqrt_fusion, f32[256]{0:T(256)S(1)} %broadcast_multiply_fusion), kind=kOutput, calls=%fused_computation.57 | convolution fusion | flops 3227910144 | bytes 15501312 | tf_op jit(solution)/shard_map/dot_general | solution.py:76
  314.7 0.0 copy-done.3
  314.7 4.0 conditional.1
  314.8 0.7 fusion.14
  315.5 0.3 copy.29
  315.7 0.7 iota_compare_fusion
  316.4 0.7 broadcast_select_fusion.1
  317.1 0.1 broadcast_and_fusion.1
  317.2 0.6 fusion.39
  317.9 0.8 convolution_convert_fusion.1
  318.7 0.0 copy-start.2
  318.7 4.9 %convolution_convert_fusion.2 = bf16[256,4096]{1,0:T(8,128)(2,1)} fusion(bf16[256,512]{0,1:T(8,128)(2,1)S(1)} %get-tuple-element.40, bf16[4096,512]{1,0:T(8,128)(2,1)} %bitcast.89), kind=kOutput, calls=%fused_computation.49 | convolution fusion | flops 1074790400 | bytes 6553600 | tf_op jit(solution)/shard_map/tr,brc->tbc/dot_general | solution.py:101
  323.6 0.0 reduce-scatter.2.cloned.1.call-update
  323.7 0.0 copy-done
  323.7 40.9 %reduce-scatter.2.cloned.1.call-done = bf16[256,512]{1,0:T(8,128)(2,1)} async-done(((bf16[256,4096]{1,0:T(8,128)(2,1)}), bf16[256,512]{1,0:T(8,128)(2,1)}) %reduce-scatter.2.cloned.1.call-update) | async-done | bytes 262160 | tf_op jit(solution)/shard_map/reduce_scatter | solution.py:104
  364.5 0.0 copy-done.2
  364.5 1.0 fusion.37
  365.6 25.7 %all_to_all.5 = bf16[16,16,512]{2,1,0:T(8,128)(2,1)S(1)} all-to-all(bf16[16,16,512]{2,1,0:T(8,128)(2,1)S(1)} %bitcast.93), channel_id=1, replica_groups=mesh['segment'=4,'zh'=2,'x'=4,'c'=2,'mp'=8] {'zh','x','c'}, dimensions={0} | all-to-all | bytes 524288 | tf_op jit(solution)/shard_map/all_to_all | solution.py:52
  391.2 4.9 %collective-permute-start = (bf16[16,16,512]{2,1,0:T(8,128)(2,1)S(1)}, bf16[16,16,512]{2,1,0:T(8,128)(2,1)S(1)}, u32[]{:S(2)}, u32[]{:S(2)}) collective-permute-start(bf16[16,16,512]{2,1,0:T(8,128)(2,1)S(1)} %all_to_all.5), channel_id=1, source_target_pairs={{0,128},{128,256},{256,384},{384,0},{1,129},{129,257},{257,385},{3... | collective-permute-start | bytes 786440 | tf_op jit(solution)/shard_map/ppermute | solution.py:14
  396.2 5.6 %collective-permute-done = bf16[16,16,512]{2,1,0:T(8,128)(2,1)S(1)} collective-permute-done((bf16[16,16,512]{2,1,0:T(8,128)(2,1)S(1)}, bf16[16,16,512]{2,1,0:T(8,128)(2,1)S(1)}, u32[]{:S(2)}, u32[]{:S(2)}) %collective-permute-start) | collective-permute-done | bytes 262176 | tf_op jit(solution)/shard_map/ppermute | solution.py:14
  401.8 0.7 copy.43
  (5 shorter events, 0.0 us)
Async XLA Ops:
  6.5 317.1 %copy-start = (f32[1,4096]{1,0:T(1,128)S(1)}, f32[1,4096]{1,0:T(1,128)}, u32[]{:S(2)}) copy-start(f32[1,4096]{1,0:T(1,128)} %param.14) | copy-start | bytes 49156
  6.5 64.8 %all-gather.14.cloned.1.call-start = ((), (), s32[]{:S(2)}) async-start(), calls=%async_computation.3 | async-start | bytes 2359296 | tf_op jit(solution)/shard_map/all_gather | solution.py:45
  7.3 98.9 %all-gather.20.cloned.1.call-start = ((), (), s32[]{:S(2)}) async-start(), calls=%async_computation.7 | async-start | bytes 2621440 | tf_op jit(solution)/shard_map/all_gather | solution.py:46
  26.9 152.4 %all-gather.16.cloned.1.call-start = ((), (), s32[]{:S(2)}) async-start(), calls=%async_computation.5 | async-start | bytes 7864320 | tf_op jit(solution)/shard_map/all_gather | solution.py:46
  71.4 150.0 %all-gather.12.cloned.1.call-start = ((), (), s32[]{:S(2)}) async-start(), calls=%async_computation.2 | async-start | bytes 2359296 | tf_op jit(solution)/shard_map/all_gather | solution.py:65
  72.0 177.5 %all-gather.22.cloned.1.call-start = ((), (), s32[]{:S(2)}) async-start(), calls=%async_computation.8 | async-start | bytes 6291456 | tf_op jit(solution)/shard_map/all_gather | solution.py:47
  106.2 179.4 %all-gather.18.cloned.1.call-start = ((), (), s32[]{:S(2)}) async-start(), calls=%async_computation.6 | async-start | bytes 18874368 | tf_op jit(solution)/shard_map/all_gather | solution.py:47
  190.8 173.8 %reduce-scatter.2.cloned.1.call-start = ((), (), s32[]{:S(2)}) async-start(), calls=%async_computation.4 | async-start | bytes 2359296 | tf_op jit(solution)/shard_map/reduce_scatter | solution.py:104
  255.9 50.7 %copy-start.1 = (bf16[1,1,256,4096]{3,2,1,0:T(8,128)(2,1)S(1)}, bf16[1,1,256,4096]{3,2,1,0:T(8,128)(2,1)}, u32[]{:S(2)}) copy-start(bf16[1,1,256,4096]{3,2,1,0:T(8,128)(2,1)} %all-gather.12.cloned.1.call-done) | copy-start | bytes 6291460
  255.9 50.7 %copy-start.4 = (f32[1,4096]{1,0:T(1,128)S(1)}, f32[1,4096]{1,0:T(1,128)}, u32[]{:S(2)}) copy-start(f32[1,4096]{1,0:T(1,128)} %param.12) | copy-start | bytes 49156
  255.9 50.7 %copy-start.5 = (f32[1,4096]{1,0:T(1,128)S(1)}, f32[1,4096]{1,0:T(1,128)}, u32[]{:S(2)}) copy-start(f32[1,4096]{1,0:T(1,128)} %param.13) | copy-start | bytes 49156
  306.6 8.1 %copy-start.3 = (s32[1,16]{1,0:T(1,128)S(1)}, s32[1,16]{1,0:T(1,128)}, u32[]{:S(2)}) copy-start(s32[1,16]{1,0:T(1,128)} %param.15) | copy-start | bytes 196
  318.7 45.8 %copy-start.2 = (bf16[1,1,256,512]{3,2,1,0:T(8,128)(2,1)S(1)}, bf16[1,1,256,512]{3,2,1,0:T(8,128)(2,1)}, u32[]{:S(2)}) copy-start(bf16[1,1,256,512]{3,2,1,0:T(8,128)(2,1)} %param.9) | copy-start | bytes 786436
  391.2 10.6 %collective-permute-start = (bf16[16,16,512]{2,1,0:T(8,128)(2,1)S(1)}, bf16[16,16,512]{2,1,0:T(8,128)(2,1)S(1)}, u32[]{:S(2)}, u32[]{:S(2)}) collective-permute-start(bf16[16,16,512]{2,1,0:T(8,128)(2,1)S(1)} %all_to_all.5), channel_id=1, source_target_pairs={{0,128},{128,256},{256,384},{384,0},{1,129},{129,257},{257,385},{3... | collective-permute-start | bytes 786440 | tf_op jit(solution)/shard_map/ppermute | solution.py:14
Sparse Core Ops, SparseCore 0:
  9.4 61.9 all-gather.13
  73.5 32.6 all-gather.19
  108.2 71.0 all-gather.15
  181.3 40.0 all-gather.11
  223.3 26.1 all-gather.21
  251.5 34.0 all-gather.17
  323.8 40.7 reduce-scatter.1
where the time goes:
time: 411 us; the launch traced here: 409 us
  waiting for transfers between devices  284 us (69%)
  blocking collectives  45.2 us (11%)
  local copies, waits for them, and re-layouts  39.8 us (10%)
  matrix products  14.4 us (4%)
  between operations  13.6 us (3%)
  other arithmetic  7.48 us (2%)
  starting transfers between devices  5.16 us (1%)
    all_gather x2, waiting for transfers between devices, gather_seq(): along = lax.all_gather(across, 'x', axis=1)  107 us
    all_gather x2, waiting for transfers between devices, gather_seq(): both = lax.all_gather(along, 'c', axis=2)  53.6 us
    all_gather x1, waiting for transfers between devices, gather_seq(): across = lax.all_gather(block, 'zh', axis=0)  44.4 us
    reduce_scatter x1, waiting for transfers between devices, on_device(): lax.psum_scatter(partials.astype(jnp.bfloat16), 'mp', scatter_dimension=1...  40.9 us
    all_gather x1, waiting for transfers between devices, on_device(): gathered = lax.all_gather(latents, 'mp', axis=3, tiled=True)[0, 0]  30.5 us
    all_to_all x1, blocking collectives, relay_features(): lax.all_to_all(rows_now, SEQ, split_axis=0, concat_axis=0, tiled=True)  25.7 us
    another operation x1, local copies, waits for them, and re-layouts, on_device(): piece.reshape(height, columns)  21 us
    all_gather x1, blocking collectives, gather_seq(): across = lax.all_gather(block, 'zh', axis=0)  19.6 us
  transfers between devices with their start and end apart: 8, of which 8 were waited for; matrix products, arithmetic and copies ran while one was open for 5% of the time, Pallas kernels for 0%

commit v1 on v0

--- a/solution.py
+++ b/solution.py
@@ -62,7 +62,9 @@
     narrow = latents.shape[3]
     span = patches // frames
     segment_rows = latents[0, 0]
-    gathered = lax.all_gather(latents, "mp", axis=3, tiled=True)[0, 0]
+    gathered = jnp.concatenate(
+        lax.all_to_all(jnp.stack([latents] * lax.axis_size("mp")), "mp", 0, 0), axis=3
+    )[0, 0]
     widened = gathered.astype(jnp.float32)
     average = jnp.mean(widened, axis=-1, keepdims=True)
     centred = widened - average

time: 411 us -> 381 us (0.927)
  waiting for transfers between devices: 284 us -> 245 us
  starting transfers between devices: 5.16 us -> 11.8 us
    all_gather x2, waiting for transfers between devices: 53.6 us -> 0.01 us  [gather_seq(): both = lax.all_gather(along, 'c', axis=2)]
    all_to_all x0 -> x1, waiting for transfers between devices: none -> 49.9 us  [on_device(): lax.all_to_all(jnp.stack([latents] * lax.axis_size('mp')), 'mp', 0, 0)]
    all_gather x1 -> x0, waiting for transfers between devices: 30.5 us -> none  [on_device(): gathered = lax.all_gather(latents, 'mp', axis=3, tiled=True)[0, 0]]
    all_to_all x0 -> x1, starting transfers between devices: none -> 6.46 us  [on_device(): lax.all_to_all(jnp.stack([latents] * lax.axis_size('mp')), 'mp', 0, 0)]
    reduce_scatter x1, waiting for transfers between devices: 40.9 us -> 36.3 us  [on_device(): lax.psum_scatter(partials.astype(jnp.bfloat16), 'mp', scatter_dimension=1...]
  transfers between devices with their start and end apart: 8 -> 8, of which waited for: 8 -> 6; matrix products, arithmetic and copies ran while one was open for 5% -> 7% of each run, Pallas kernels for 0% -> 0%
where the time goes in v1:
time: 381 us; the launch traced here: 380 us
  waiting for transfers between devices  245 us (64%)
  blocking collectives  45.5 us (12%)
  local copies, waits for them, and re-layouts  43 us (11%)
  between operations  13.6 us (4%)
  matrix products  12.9 us (3%)
  starting transfers between devices  11.8 us (3%)
  other arithmetic  8.2 us (2%)
    all_gather x2, waiting for transfers between devices, gather_seq(): along = lax.all_gather(across, 'x', axis=1)  108 us
    all_to_all x1, waiting for transfers between devices, on_device(): lax.all_to_all(jnp.stack([latents] * lax.axis_size('mp')), 'mp', 0, 0)  49.9 us
    all_gather x1, waiting for transfers between devices, gather_seq(): across = lax.all_gather(block, 'zh', axis=0)  44.4 us
    reduce_scatter x1, waiting for transfers between devices, on_device(): lax.psum_scatter(partials.astype(jnp.bfloat16), 'mp', scatter_dimension=1...  36.3 us
    all_to_all x1, blocking collectives, relay_features(): lax.all_to_all(rows_now, SEQ, split_axis=0, concat_axis=0, tiled=True)  26 us
    another operation x1, local copies, waits for them, and re-layouts, on_device(): piece.reshape(height, columns)  21.1 us
    all_gather x1, blocking collectives, gather_seq(): across = lax.all_gather(block, 'zh', axis=0)  19.6 us
    all_gather x1, local copies, waits for them, and re-layouts, gather_seq(): along = lax.all_gather(across, 'x', axis=1)  11.4 us
  transfers between devices with their start and end apart: 8, of which 6 were waited for; matrix products, arithmetic and copies ran while one was open for 7% of the time, Pallas kernels for 0%

profile of v1, /device:TPU:1, one launch (start us, length us, event | category | flops | bytes accessed | tf_op | source)
XLA Modules:
  0.0 379.8 jit_solution(12474662875677199753)
XLA Ops:
  6.5 0.0 copy-start
  6.5 0.0 all-gather.11.cloned.1.call-start
  6.5 0.7 all-gather.11.cloned.1.call-update
  7.3 0.0 all-gather.17.cloned.1.call-start
  7.3 19.6 %all-gather.2 = bf16[2,512,256]{2,1,0:T(8,128)(2,1)} all-gather(bf16[1,512,256]{2,1,0:T(8,128)(2,1)} %param.11), channel_id=4, replica_groups=mesh['segment'=4,'zh'=2,'x'=4,'c'=2,'mp'=8] {'zh'}, dimensions={0}, use_global_device_ids=true | all-gather | bytes 786432 | tf_op jit(solution)/shard_map/all_gather | solution.py:45
  26.9 0.0 all-gather.17.cloned.1.call-update
  26.9 0.0 all-gather.13.cloned.1.call-start
  26.9 44.4 %all-gather.11.cloned.1.call-done = bf16[2,256,3,512]{3,1,2,0:T(8,128)(2,1)} async-done(((bf16[1,256,3,512]{3,1,2,0:T(8,128)(2,1)}), bf16[2,256,3,512]{3,1,2,0:T(8,128)(2,1)}) %all-gather.11.cloned.1.call-update) | async-done | bytes 1572880 | tf_op jit(solution)/shard_map/all_gather | solution.py:45
  71.4 0.0 all-gather.13.cloned.1.call-update
  71.4 0.0 all-gather.19.cloned.1.call-start
  71.4 34.7 %all-gather.17.cloned.1.call-done = bf16[2,2048,256]{2,1,0:T(8,128)(2,1)} async-done(((bf16[2,512,256]{2,1,0:T(8,128)(2,1)}), bf16[2,2048,256]{2,1,0:T(8,128)(2,1)}) %all-gather.17.cloned.1.call-update) | async-done | bytes 2097168 | tf_op jit(solution)/shard_map/all_gather | solution.py:46
  106.1 0.0 all-gather.19.cloned.1.call-update
  106.2 0.0 all-gather.15.cloned.1.call-start
  106.2 73.1 %all-gather.13.cloned.1.call-done = bf16[2,1024,3,512]{3,1,2,0:T(8,128)(2,1)} async-done(((bf16[2,256,3,512]{3,1,2,0:T(8,128)(2,1)}), bf16[2,1024,3,512]{3,1,2,0:T(8,128)(2,1)}) %all-gather.13.cloned.1.call-update) | async-done | bytes 6291472 | tf_op jit(solution)/shard_map/all_gather | solution.py:46
  179.3 11.4 %copy.31 = bf16[2,4,256,3,512]{2,1,0,4,3:T(4,128)(2,1)} copy(bf16[2,4,256,3,512]{4,2,1,3,0:T(8,128)(2,1)} %bitcast.84) | data formatting | bytes 12582912 | tf_op jit(solution)/shard_map/all_gather | solution.py:46
  190.8 0.0 copy-start.2
  190.8 0.0 all-gather.15.cloned.1.call-update
  190.8 0.0 copy-start.3
  190.8 0.0 copy-start.4
  190.8 0.9 copy-done.2
  191.7 0.1 copy.29
  191.8 1.5 stack.2
  193.4 6.5 %all-to-all-start = ((bf16[8,1,1,256,512]{3,4,2,1,0:T(8,128)(2,1)}), bf16[8,1,1,256,512]{3,4,2,1,0:T(8,128)(2,1)S(1)}, u32[]{:S(2)}, u32[]{:S(2)}) async-start(bf16[8,1,1,256,512]{3,4,2,1,0:T(8,128)(2,1)} %stack.2), calls=%async_computation | async-start | bytes 4194304 | tf_op jit(solution)/shard_map/all_to_all | solution.py:66
  199.8 0.0 reduce-scatter.2.cloned.1.call-start
  199.9 0.5 broadcast.210
  200.4 0.0 copy-done.3
  200.4 0.6 reduce.10
  201.0 0.0 copy-done.4
  201.0 0.6 reduce.11
  201.6 49.9 %all-to-all-done = bf16[8,1,1,256,512]{3,4,2,1,0:T(8,128)(2,1)S(1)} async-done(((bf16[8,1,1,256,512]{3,4,2,1,0:T(8,128)(2,1)}), bf16[8,1,1,256,512]{3,4,2,1,0:T(8,128)(2,1)S(1)}, u32[]{:S(2)}, u32[]{:S(2)}) %all-to-all-start) | async-done | bytes 2097184 | tf_op jit(solution)/shard_map/all_to_all | solution.py:66
  251.5 0.6 convert_reduce_fusion
  252.1 0.6 fusion.26
  252.7 2.7 fusion.29
  255.3 0.0 all-gather.19.cloned.1.call-done
  255.3 6.4 %copy.33 = bf16[16,256,512]{2,1,0:T(8,128)(2,1)} copy(bf16[16,256,512]{1,2,0:T(8,128)(2,1)} %bitcast.85) | data formatting | bytes 8388608 | tf_op jit(solution)/shard_map/tr,brc->tbc/dot_general | solution.py:103
  261.7 0.0 copy-start.1
  261.7 0.0 all-gather.15.cloned.1.call-done
  261.7 21.1 %reshape_reshape.6 = bf16[4096,1536]{0,1:T(8,128)(2,1)} reshape(bf16[2,4,512,3,512]{2,1,0,4,3:T(4,128)(2,1)} %all-gather.15.cloned.1.call-done) | data formatting | bytes 25165824 | tf_op jit(solution)/shard_map/reshape;reshape | solution.py:79
  282.9 0.0 copy-done.1
  282.9 0.0 copy-start.5
  282.9 6.6 %convolution_convert_fusion.3 = bf16[256,1536]{1,0:T(8,128)(2,1)S(1)} fusion(bf16[256,4096]{0,1:T(8,128)(2,1)S(1)} %bitcast.87, bf16[4096,1536]{0,1:T(8,128)(2,1)} %reshape_reshape.6), kind=kOutput, calls=%fused_computation.55 | convolution fusion | flops 3221618688 | bytes 15466496 | tf_op jit(solution)/shard_map/dot_general | solution.py:78
  289.5 0.0 copy-done.5
  289.5 4.0 %conditional.1 = (bf16[256,512]{0,1:T(8,128)(2,1)S(1)}) conditional(s32[]{:T(128)} %convert_element_type.51, (s32[]{:T(128)}, s32[1,16]{1,0:T(1,128)S(1)}, bf16[256,1536]{1,0:T(8,128)(2,1)S(1)}) %tuple.31, (s32[]{:T(128)}, s32[16]{0:T(128)S(1)}, s32[1,16]{1,0:T(1,128)S(1)}, bf16[256,1536]{1,0:T(8,128)(2,1)S(1)}) %tuple.32), branch_computations={%region_2.5_spmd, %region_5.9_spmd} | conditional | flops 204410160 | bytes 6552408 | solution.py:99
  289.5 0.7 fusion.14
  290.2 0.3 copy.32
  290.5 0.7 iota_compare_fusion
  291.2 0.7 broadcast_select_fusion.1
  291.9 0.1 broadcast_and_fusion.1
  292.0 0.6 fusion.31
  292.6 0.8 convolution_convert_fusion.1
  293.5 4.9 %convolution_convert_fusion.2 = bf16[256,4096]{1,0:T(8,128)(2,1)} fusion(bf16[256,512]{0,1:T(8,128)(2,1)S(1)} %get-tuple-element.40, bf16[4096,512]{1,0:T(8,128)(2,1)} %bitcast.83), kind=kOutput, calls=%fused_computation.48 | convolution fusion | flops 1074790400 | bytes 6553600 | tf_op jit(solution)/shard_map/tr,brc->tbc/dot_general | solution.py:103
  298.3 0.0 reduce-scatter.2.cloned.1.call-update
  298.4 0.0 copy-done
  298.4 36.3 %reduce-scatter.2.cloned.1.call-done = bf16[256,512]{1,0:T(8,128)(2,1)} async-done(((bf16[256,4096]{1,0:T(8,128)(2,1)}), bf16[256,512]{1,0:T(8,128)(2,1)}) %reduce-scatter.2.cloned.1.call-update) | async-done | bytes 262160 | tf_op jit(solution)/shard_map/reduce_scatter | solution.py:106
  334.7 1.0 add_convert_fusion
  335.7 26.0 %all_to_all.10 = bf16[16,16,512]{2,1,0:T(8,128)(2,1)S(1)} all-to-all(bf16[16,16,512]{2,1,0:T(8,128)(2,1)S(1)} %bitcast.89), channel_id=1, replica_groups=mesh['segment'=4,'zh'=2,'x'=4,'c'=2,'mp'=8] {'zh','x','c'}, dimensions={0} | all-to-all | bytes 524288 | tf_op jit(solution)/shard_map/all_to_all | solution.py:52
  361.7 5.1 %collective-permute-start = (bf16[16,16,512]{2,1,0:T(8,128)(2,1)S(1)}, bf16[16,16,512]{2,1,0:T(8,128)(2,1)S(1)}, u32[]{:S(2)}, u32[]{:S(2)}) collective-permute-start(bf16[16,16,512]{2,1,0:T(8,128)(2,1)S(1)} %all_to_all.10), channel_id=1, source_target_pairs={{0,128},{128,256},{256,384},{384,0},{1,129},{129,257},{257,385},{3... | collective-permute-start | bytes 786440 | tf_op jit(solution)/shard_map/ppermute | solution.py:14
  366.8 5.4 %collective-permute-done = bf16[16,16,512]{2,1,0:T(8,128)(2,1)S(1)} collective-permute-done((bf16[16,16,512]{2,1,0:T(8,128)(2,1)S(1)}, bf16[16,16,512]{2,1,0:T(8,128)(2,1)S(1)}, u32[]{:S(2)}, u32[]{:S(2)}) %collective-permute-start) | collective-permute-done | bytes 262176 | tf_op jit(solution)/shard_map/ppermute | solution.py:14
  372.2 0.7 copy.46
  (7 shorter events, 0.0 us)
Async XLA Ops:
  6.5 291.8 %copy-start = (f32[1,4096]{1,0:T(1,128)S(1)}, f32[1,4096]{1,0:T(1,128)}, u32[]{:S(2)}) copy-start(f32[1,4096]{1,0:T(1,128)} %param.14) | copy-start | bytes 49156
  6.5 64.8 %all-gather.11.cloned.1.call-start = ((), (), s32[]{:S(2)}) async-start(), calls=%async_computation.3 | async-start | bytes 2359296 | tf_op jit(solution)/shard_map/all_gather | solution.py:45
  7.3 98.9 %all-gather.17.cloned.1.call-start = ((), (), s32[]{:S(2)}) async-start(), calls=%async_computation.7 | async-start | bytes 2621440 | tf_op jit(solution)/shard_map/all_gather | solution.py:46
  26.9 152.4 %all-gather.13.cloned.1.call-start = ((), (), s32[]{:S(2)}) async-start(), calls=%async_computation.5 | async-start | bytes 7864320 | tf_op jit(solution)/shard_map/all_gather | solution.py:46
  71.4 183.9 %all-gather.19.cloned.1.call-start = ((), (), s32[]{:S(2)}) async-start(), calls=%async_computation.8 | async-start | bytes 6291456 | tf_op jit(solution)/shard_map/all_gather | solution.py:47
  106.2 155.6 %all-gather.15.cloned.1.call-start = ((), (), s32[]{:S(2)}) async-start(), calls=%async_computation.6 | async-start | bytes 18874368 | tf_op jit(solution)/shard_map/all_gather | solution.py:47
  190.8 0.9 copy-start.2
  190.8 9.6 %copy-start.3 = (f32[1,4096]{1,0:T(1,128)S(1)}, f32[1,4096]{1,0:T(1,128)}, u32[]{:S(2)}) copy-start(f32[1,4096]{1,0:T(1,128)} %param.12) | copy-start | bytes 49156
  190.8 10.2 %copy-start.4 = (f32[1,4096]{1,0:T(1,128)S(1)}, f32[1,4096]{1,0:T(1,128)}, u32[]{:S(2)}) copy-start(f32[1,4096]{1,0:T(1,128)} %param.13) | copy-start | bytes 49156
  193.4 58.1 %all-to-all-start = ((bf16[8,1,1,256,512]{3,4,2,1,0:T(8,128)(2,1)}), bf16[8,1,1,256,512]{3,4,2,1,0:T(8,128)(2,1)S(1)}, u32[]{:S(2)}, u32[]{:S(2)}) async-start(bf16[8,1,1,256,512]{3,4,2,1,0:T(8,128)(2,1)} %stack.2), calls=%async_computation | async-start | bytes 4194304 | tf_op jit(solution)/shard_map/all_to_all | solution.py:66
  199.8 134.8 %reduce-scatter.2.cloned.1.call-start = ((), (), s32[]{:S(2)}) async-start(), calls=%async_computation.4 | async-start | bytes 2359296 | tf_op jit(solution)/shard_map/reduce_scatter | solution.py:106
  261.7 21.1 %copy-start.1 = (bf16[8,1,1,256,512]{3,4,0,2,1:T(8,128)(2,1)S(1)}, bf16[8,1,1,256,512]{3,4,0,2,1:T(8,128)(2,1)}, u32[]{:S(2)}) copy-start(bf16[8,1,1,256,512]{3,4,0,2,1:T(8,128)(2,1)} %fusion.29) | copy-start | bytes 6291460
  282.9 6.6 %copy-start.5 = (s32[1,16]{1,0:T(1,128)S(1)}, s32[1,16]{1,0:T(1,128)}, u32[]{:S(2)}) copy-start(s32[1,16]{1,0:T(1,128)} %param.15) | copy-start | bytes 196
  361.7 10.6 %collective-permute-start = (bf16[16,16,512]{2,1,0:T(8,128)(2,1)S(1)}, bf16[16,16,512]{2,1,0:T(8,128)(2,1)S(1)}, u32[]{:S(2)}, u32[]{:S(2)}) collective-permute-start(bf16[16,16,512]{2,1,0:T(8,128)(2,1)S(1)} %all_to_all.10), channel_id=1, source_target_pairs={{0,128},{128,256},{256,384},{384,0},{1,129},{129,257},{257,385},{3... | collective-permute-start | bytes 786440 | tf_op jit(solution)/shard_map/ppermute | solution.py:14
Sparse Core Ops, SparseCore 0:
  9.4 61.9 all-gather.10
  73.5 32.6 all-gather.16
  108.2 71.0 all-gather.12
  181.3 24.1 all-gather.18
  207.4 34.0 all-gather.14
  298.5 36.1 reduce-scatter.1
